TPU v7x, 32 devices: a whole 2x2x4 slice. The times are simulated.
32 devices in a mesh: groups: 2 (over y), dp: 4 (over z), tensor: 2 (over x), layer: 2 (over core).
Axes of the slice: x: 2, y: 2, z: 4, core: 2. Of those that a mesh axis runs over, the one named last changes fastest.
Arguments:
- hidden_in: bfloat16 [2, 8, 512, 14336], P('layer', ('groups', 'dp'), None, 'tensor'), parts along dimension 1, may hold values from -6 to 6
- out_grad: bfloat16 [2, 8, 512, 4096], P('layer', ('groups', 'dp'), 'tensor'), parts along dimension 1, may hold values from -6 to 6
- proj_in: bfloat16 [2, 14336, 64], P('layer', 'tensor'), may hold values from -0.046875 to 0.046875
- proj_out: bfloat16 [2, 4096, 64], P('layer'), may hold values from -0.09375 to 0.09375
- query_grads: bfloat16 [2, 1024, 4096], P('layer', 'dp', 'tensor'), may hold values from -1.5 to 1.5
- lengths: int32 [8], P(('groups', 'dp')), parts along dimension 0, may hold values from 128 to 512, as said below
- query_decision: int32 [1024], P('dp'), may hold values from 0 to 1023
Outputs:
- influence: float32 [8, 1024], P(('groups', 'dp')), parts along dimension 0
There are 2 independent parts, one for each index of `groups`. A program takes and returns all parts, laid end to end along the dimension named above; an argument that names none is the same for every part. Nothing has to cross between parts.
Inputs may be any that keep to these rules, and one draw needn't show every extreme that they name: `lengths`: in each part one transcript has all 512 tokens live and another has exactly 128.
All inputs are finite; a program needn't handle non-finite values.
Results may differ from a plain program's by a relative error of at most 0.004.
Values may be sent and summed in bfloat16 or wider, within the bound.
No kernel may reach another device: no remote copies, remote signals or barrier semaphores. Data moves between devices by JAX's collectives and lax.ppermute only.
A program may use at most 64 MiB of HBM per device.

v0:
```python
import jax
import jax.numpy as jnp
from jax import lax
from jax.sharding import PartitionSpec as P

DECISIONS = 1024


def body(hidden_in, out_grad, proj_in, proj_out, query_grads, lengths, query_decision):
    hidden_rows = hidden_in[0, 0]
    grad_rows = out_grad[0, 0]
    side_hidden = proj_in[0]
    side_width = proj_out[0]
    query_rows = query_grads[0]
    length = lengths[0]
    seq_shard = grad_rows.shape[0]
    first_pos = lax.axis_index("tensor") * seq_shard
    positions = first_pos + jnp.arange(seq_shard, dtype=jnp.int32)
    live = (positions < length).astype(jnp.float32)
    right = jnp.dot(grad_rows, side_width, preferred_element_type=jnp.float32)
    right = (right * live[:, None]).astype(jnp.bfloat16)
    right_full = lax.all_gather(right, "tensor", axis=0, tiled=True)
    left = jnp.dot(hidden_rows, side_hidden, preferred_element_type=jnp.float32)
    partial = jnp.dot(left.T, right_full.astype(jnp.float32), precision=lax.Precision.HIGHEST)
    partial = partial / length.astype(jnp.float32)
    grad_part = lax.psum_scatter(partial, "tensor", scatter_dimension=0, tiled=True)
    grad_flat = grad_part.reshape(1, -1).astype(jnp.bfloat16)
    grads_all = lax.all_gather(grad_flat, "dp", axis=0, tiled=True)
    scores = jnp.dot(grads_all, query_rows.T, preferred_element_type=jnp.float32)
    table = (query_decision[:, None] == jnp.arange(DECISIONS, dtype=jnp.int32)[None, :]).astype(
        jnp.float32
    )
    partial_dec = jnp.dot(scores, table, precision=lax.Precision.HIGHEST)
    total = lax.psum(partial_dec, ("dp", "tensor", "layer"))
    row = lax.dynamic_slice_in_dim(total, lax.axis_index("dp"), 1, axis=0)
    return row


def solution(mesh):
    in_specs = (
        P("layer", ("groups", "dp"), None, "tensor"),
        P("layer", ("groups", "dp"), "tensor", None),
        P("layer", "tensor", None),
        P("layer", None, None),
        P("layer", "dp", "tensor"),
        P(("groups", "dp")),
        P("dp"),
    )
    out_specs = P(("groups", "dp"), None)
    return jax.shard_map(body, mesh=mesh, in_specs=in_specs, out_specs=out_specs, check_vma=False)
```

profile of v0, /device:TPU:0, one launch (start us, length us, event | category | flops | bytes accessed | tf_op | source)
XLA Modules:
  0.0 113.7 jit_solution(15606715019655168779)
XLA Ops:
  6.5 0.0 copy-start
  6.5 0.0 copy-start.1
  6.5 0.0 copy-start.2
  6.5 0.0 reduce-scatter.2.cloned.1.call-start
  7.4 0.8 copy-done
  8.1 1.8 %fusion.7 = bf16[256,64]{0,1:T(8,128)(2,1)S(1)} fusion(bf16[1,1,256,4096]{3,2,1,0:T(8,128)(2,1)S(1)} %copy-done, bf16[1,4096,64]{1,2,0:T(8,128)(2,1)} %param.10, f32[256]{0:T(256)S(1)} %compare_convert_fusion), kind=kOutput, calls=%fused_computation.5 | convolution fusion | flops 134250496 | bytes 2655232 | tf_op jit(solution)/shard_map/dot_general | solution.py:20
  9.9 5.5 %all_gather.6 = bf16[512,64]{0,1:T(8,128)(2,1)S(1)} all-gather(bf16[256,64]{0,1:T(8,128)(2,1)S(1)} %fusion.7), channel_id=1, replica_groups=mesh['groups'=2,'dp'=4,'tensor'=2,'layer'=2] {'tensor'}, dimensions={0}, use_global_device_ids=true | all-gather | bytes 98304 | tf_op jit(solution)/shard_map/all_gather | solution.py:22
  15.5 5.6 %fusion = f32[512,64]{0,1:T(8,128)S(1)} fusion(bf16[1,1,512,7168]{3,2,1,0:T(8,128)(2,1)} %param.7, bf16[1,7168,64]{1,2,0:T(8,128)(2,1)} %param.9), kind=kOutput, calls=%fused_computation | convolution fusion | flops 469762048 | bytes 8388608 | tf_op jit(solution)/shard_map/dot_general | solution.py:23
  21.1 0.8 convolution_divide_fusion
  21.9 0.0 reduce-scatter.2.cloned.1.call-update
  21.9 11.9 %reduce-scatter.2.cloned.1.call-done = f32[32,64]{1,0:T(8,128)} async-done(((f32[64,64]{1,0:T(8,128)}), f32[32,64]{1,0:T(8,128)}) %reduce-scatter.2.cloned.1.call-update) | async-done | bytes 8208 | tf_op jit(solution)/shard_map/reduce_scatter | solution.py:26
  33.8 0.7 convert_element_type.32
  34.5 0.1 reshape.21
  34.6 13.2 %all-gather = bf16[4,1,2048]{2,1,0:T(2,128)(2,1)S(1)} all-gather(bf16[1,1,2048]{2,1,0:T(2,128)(2,1)S(1)} %reshape.21), channel_id=1, replica_groups=mesh['groups'=2,'dp'=4,'tensor'=2,'layer'=2] {'dp'}, dimensions={0}, use_global_device_ids=true | all-gather | bytes 20480 | tf_op jit(solution)/shard_map/all_gather | solution.py:28
  47.8 0.0 copy-done.1
  47.8 0.4 fusion.10
  48.2 0.0 copy-done.2
  48.2 0.5 fusion.12
  48.7 57.6 %psum.7 = f32[4,1024]{1,0:T(4,128)S(1)} all-reduce(f32[4,1024]{1,0:T(4,128)S(1)} %fusion.12), channel_id=1, replica_groups=mesh['groups'=2,'dp'=4,'tensor'=2,'layer'=2] {'dp','tensor','layer'}, use_global_device_ids=true, to_apply=%region_1.0 | all-reduce | flops 4096 | bytes 32768 | tf_op jit(solution)/shard_map/psum | solution.py:34
  106.3 0.6 constant_dynamic-slice_fusion
  (1 shorter events, 0.0 us)
Async XLA Ops:
  6.5 1.6 %copy-start = (bf16[1,1,256,4096]{3,2,1,0:T(8,128)(2,1)S(1)}, bf16[1,1,256,4096]{3,2,1,0:T(8,128)(2,1)}, u32[]{:S(2)}) copy-start(bf16[1,1,256,4096]{3,2,1,0:T(8,128)(2,1)} %param.8) | copy-start | bytes 6291460
  6.5 41.2 %copy-start.1 = (bf16[1,256,2048]{2,1,0:T(8,128)(2,1)S(1)}, bf16[1,256,2048]{2,1,0:T(8,128)(2,1)}, u32[]{:S(2)}) copy-start(bf16[1,256,2048]{2,1,0:T(8,128)(2,1)} %param.11) | copy-start | bytes 3145732
  6.5 41.6 %copy-start.2 = (s32[256]{0:T(256)S(1)}, s32[256]{0:T(256)}, u32[]{:S(2)}) copy-start(s32[256]{0:T(256)} %param.13) | copy-start | bytes 3076
  6.5 27.3 %reduce-scatter.2.cloned.1.call-start = ((), (), s32[]{:S(2)}) async-start(), calls=%async_computation.1 | async-start | bytes 49152 | tf_op jit(solution)/shard_map/reduce_scatter | solution.py:26
Sparse Core Ops, SparseCore 0:
  22.0 11.7 reduce-scatter.1
where the time goes:
time: 114 us
  blocking collectives  76.3 us (67%)
  between operations  14.2 us (12%)
  waiting for transfers between devices  11.9 us (10%)
  matrix products  9.12 us (8%)
  local copies, waits for them, and re-layouts  1.48 us (1%)
    psum x1, blocking collectives, body(): total = lax.psum(partial_dec, ('dp', 'tensor', 'layer'))  57.6 us
    all_gather x1, blocking collectives, body(): grads_all = lax.all_gather(grad_flat, 'dp', axis=0, tiled=True)  13.2 us
    reduce_scatter x1, waiting for transfers between devices, body(): lax.psum_scatter(partial, 'tensor', scatter_dimension=0, tiled=True)  11.9 us
    dot_general x1, matrix products, body(): left = jnp.dot(hidden_rows, side_hidden, preferred_element_type=jnp.float32)  5.61 us
    all_gather x1, blocking collectives, body(): right_full = lax.all_gather(right, 'tensor', axis=0, tiled=True)  5.51 us
  transfers between devices with their start and end apart: 1, of which 1 were waited for; matrix products, arithmetic and copies ran while one was open for 0% of the time, Pallas kernels for 0%

commit v1 on v0

--- a/solution.py
+++ b/solution.py
@@ -1,9 +1,28 @@
+import functools
 import jax
 import jax.numpy as jnp
 from jax import lax
 from jax.sharding import PartitionSpec as P
 
 DECISIONS = 1024
+
+
+def indices_treat(local_block, mesh_ax):
+    local_now = lax.axis_index(mesh_ax)
+    a_next = lax.axis_size(mesh_ax)
+    current_value, block_out = (a_next, local_now)
+    x_now, moved = (local_block, 1)
+    while moved < current_value:
+        long_array = tuple(((kk, kk ^ moved) for kk in range(current_value)))
+        big = lax.ppermute(x_now, mesh_ax, perm=long_array)
+        f_next = jnp.concatenate([x_now, big], 0)
+        finding = jnp.concatenate([big, x_now], 0)
+        x_now = jnp.where(block_out & moved == 0, f_next, finding)
+        moved = 2 * moved
+    return x_now
+
+
+switch_arrays = functools.partial(indices_treat, mesh_ax="dp")
 
 
 def body(hidden_in, out_grad, proj_in, proj_out, query_grads, lengths, query_decision):
@@ -25,7 +44,7 @@
     partial = partial / length.astype(jnp.float32)
     grad_part = lax.psum_scatter(partial, "tensor", scatter_dimension=0, tiled=True)
     grad_flat = grad_part.reshape(1, -1).astype(jnp.bfloat16)
-    grads_all = lax.all_gather(grad_flat, "dp", axis=0, tiled=True)
+    grads_all = switch_arrays(grad_flat)
     scores = jnp.dot(grads_all, query_rows.T, preferred_element_type=jnp.float32)
     table = (query_decision[:, None] == jnp.arange(DECISIONS, dtype=jnp.int32)[None, :]).astype(
         jnp.float32

time: 114 us -> 109 us (0.956)
  blocking collectives: 76.3 us -> 63.5 us
  waiting for transfers between devices: 11.9 us -> 16.2 us
  starting transfers between devices: 0.01 us -> 3.96 us
    all_gather x1 -> x0, blocking collectives: 13.2 us -> none  [body(): grads_all = lax.all_gather(grad_flat, 'dp', axis=0, tiled=True)]
    ppermute x0 -> x2, waiting for transfers between devices: none -> 4.31 us  [indices_treat(): big = lax.ppermute(x_now, mesh_ax, perm=long_array)]
    ppermute x0 -> x2, starting transfers between devices: none -> 3.96 us  [indices_treat(): big = lax.ppermute(x_now, mesh_ax, perm=long_array)]
  transfers between devices with their start and end apart: 1 -> 3, of which waited for: 1 -> 3; matrix products, arithmetic and copies ran while one was open for 0% -> 0% of each run, Pallas kernels for 0% -> 0%
where the time goes in v1:
time: 109 us
  blocking collectives  63.5 us (58%)
  waiting for transfers between devices  16.2 us (15%)
  between operations  14.2 us (13%)
  matrix products  8.91 us (8%)
  starting transfers between devices  3.96 us (4%)
  local copies, waits for them, and re-layouts  1.48 us (1%)
    psum x1, blocking collectives, body(): total = lax.psum(partial_dec, ('dp', 'tensor', 'layer'))  57.6 us
    reduce_scatter x1, waiting for transfers between devices, body(): lax.psum_scatter(partial, 'tensor', scatter_dimension=0, tiled=True)  11.9 us
    all_gather x1, blocking collectives, body(): right_full = lax.all_gather(right, 'tensor', axis=0, tiled=True)  5.86 us
    dot_general x1, matrix products, body(): left = jnp.dot(hidden_rows, side_hidden, preferred_element_type=jnp.float32)  5.3 us
    ppermute x2, waiting for transfers between devices, indices_treat(): big = lax.ppermute(x_now, mesh_ax, perm=long_array)  4.31 us
    ppermute x2, starting transfers between devices, indices_treat(): big = lax.ppermute(x_now, mesh_ax, perm=long_array)  3.96 us
  transfers between devices with their start and end apart: 3, of which 3 were waited for; matrix products, arithmetic and copies ran while one was open for 0% of the time, Pallas kernels for 0%

profile of v1, /device:TPU:0, one launch (start us, length us, event | category | flops | bytes accessed | tf_op | source)
XLA Modules:
  0.0 109.1 jit_solution(2589841993983319861)
XLA Ops:
  6.5 0.0 copy-start
  6.5 0.0 copy-start.1
  6.5 0.0 copy-start.2
  6.5 0.0 reduce-scatter.2.cloned.1.call-start
  7.4 0.8 copy-done
  8.1 1.7 %fusion.7 = bf16[256,64]{1,0:T(8,128)(2,1)S(1)} fusion(bf16[1,1,256,4096]{3,2,1,0:T(8,128)(2,1)S(1)} %copy-done, bf16[1,4096,64]{1,2,0:T(8,128)(2,1)} %param.10, f32[256]{0:T(256)S(1)} %compare_convert_fusion), kind=kOutput, calls=%fused_computation.5 | convolution fusion | flops 134250496 | bytes 2655232 | tf_op jit(solution)/shard_map/dot_general | solution.py:39
  9.9 5.9 %all_gather.3 = bf16[512,64]{1,0:T(8,128)(2,1)S(1)} all-gather(bf16[256,64]{1,0:T(8,128)(2,1)S(1)} %fusion.7), channel_id=1, replica_groups=mesh['groups'=2,'dp'=4,'tensor'=2,'layer'=2] {'tensor'}, dimensions={0}, use_global_device_ids=true | all-gather | bytes 98304 | tf_op jit(solution)/shard_map/all_gather | solution.py:41
  15.7 5.3 %fusion = f32[512,64]{1,0:T(8,128)S(1)} fusion(bf16[1,1,512,7168]{3,2,1,0:T(8,128)(2,1)} %param.7, bf16[1,7168,64]{1,2,0:T(8,128)(2,1)} %param.9), kind=kOutput, calls=%fused_computation | convolution fusion | flops 469762048 | bytes 8388608 | tf_op jit(solution)/shard_map/dot_general | solution.py:42
  21.1 1.0 convolution_divide_fusion
  22.0 0.0 reduce-scatter.2.cloned.1.call-update
  22.1 11.9 %reduce-scatter.2.cloned.1.call-done = f32[32,64]{1,0:T(8,128)} async-done(((f32[64,64]{1,0:T(8,128)}), f32[32,64]{1,0:T(8,128)}) %reduce-scatter.2.cloned.1.call-update) | async-done | bytes 8208 | tf_op jit(solution)/shard_map/reduce_scatter | solution.py:45
  34.0 0.7 convert_element_type.32
  34.7 0.1 convert_element_type.33
  34.8 1.5 %collective-permute-start = (bf16[1,2048]{1,0:T(2,128)(2,1)S(1)}, bf16[1,2048]{1,0:T(2,128)(2,1)S(1)}, u32[]{:S(2)}, u32[]{:S(2)}) collective-permute-start(bf16[1,2048]{1,0:T(2,128)(2,1)S(1)} %convert_element_type.33), channel_id=1, source_target_pairs={{0,4},{4,0},{8,12},{12,8},{1,5},{5,1},{9,13},{13,9},{2,6},{6,2},{1... | collective-permute-start | bytes 12296 | tf_op jit(solution)/shard_map/ppermute | solution.py:17
  36.3 2.2 %collective-permute-done = bf16[1,2048]{1,0:T(2,128)(2,1)S(1)} collective-permute-done((bf16[1,2048]{1,0:T(2,128)(2,1)S(1)}, bf16[1,2048]{1,0:T(2,128)(2,1)S(1)}, u32[]{:S(2)}, u32[]{:S(2)}) %collective-permute-start) | collective-permute-done | bytes 4128 | tf_op jit(solution)/shard_map/ppermute | solution.py:17
  38.5 2.5 %collective-permute-start.1 = (bf16[2,2048]{1,0:T(2,128)(2,1)S(1)}, bf16[2,2048]{1,0:T(2,128)(2,1)S(1)}, u32[]{:S(2)}, u32[]{:S(2)}) collective-permute-start(bf16[2,2048]{1,0:T(2,128)(2,1)S(1)} %broadcast_select_fusion), channel_id=1, source_target_pairs={{0,8},{4,12},{8,0},{12,4},{1,9},{5,13},{9,1},{13,5},{2,10},{6,14},... | collective-permute-start | bytes 24584 | tf_op jit(solution)/shard_map/ppermute | solution.py:17
  41.0 2.1 %collective-permute-done.1 = bf16[2,2048]{1,0:T(2,128)(2,1)S(1)} collective-permute-done((bf16[2,2048]{1,0:T(2,128)(2,1)S(1)}, bf16[2,2048]{1,0:T(2,128)(2,1)S(1)}, u32[]{:S(2)}, u32[]{:S(2)}) %collective-permute-start.1) | collective-permute-done | bytes 8224 | tf_op jit(solution)/shard_map/ppermute | solution.py:17
  43.1 0.0 copy-done.1
  43.1 0.4 fusion.10
  43.5 0.0 copy-done.2
  43.5 0.5 fusion.12
  44.0 57.6 %psum.7 = f32[4,1024]{1,0:T(4,128)S(1)} all-reduce(f32[4,1024]{1,0:T(4,128)S(1)} %fusion.12), channel_id=1, replica_groups=mesh['groups'=2,'dp'=4,'tensor'=2,'layer'=2] {'dp','tensor','layer'}, use_global_device_ids=true, to_apply=%region_1.2 | all-reduce | flops 4096 | bytes 32768 | tf_op jit(solution)/shard_map/psum | solution.py:53
  101.6 0.6 constant_dynamic-slice_fusion
  (2 shorter events, 0.0 us)
Async XLA Ops:
  6.5 1.6 %copy-start = (bf16[1,1,256,4096]{3,2,1,0:T(8,128)(2,1)S(1)}, bf16[1,1,256,4096]{3,2,1,0:T(8,128)(2,1)}, u32[]{:S(2)}) copy-start(bf16[1,1,256,4096]{3,2,1,0:T(8,128)(2,1)} %param.8) | copy-start | bytes 6291460
  6.5 36.6 %copy-start.1 = (bf16[1,256,2048]{2,1,0:T(8,128)(2,1)S(1)}, bf16[1,256,2048]{2,1,0:T(8,128)(2,1)}, u32[]{:S(2)}) copy-start(bf16[1,256,2048]{2,1,0:T(8,128)(2,1)} %param.11) | copy-start | bytes 3145732
  6.5 36.9 %copy-start.2 = (s32[256]{0:T(256)S(1)}, s32[256]{0:T(256)}, u32[]{:S(2)}) copy-start(s32[256]{0:T(256)} %param.13) | copy-start | bytes 3076
  6.5 27.4 %reduce-scatter.2.cloned.1.call-start = ((), (), s32[]{:S(2)}) async-start(), calls=%async_computation.1 | async-start | bytes 49152 | tf_op jit(solution)/shard_map/reduce_scatter | solution.py:45
  34.8 3.7 %collective-permute-start = (bf16[1,2048]{1,0:T(2,128)(2,1)S(1)}, bf16[1,2048]{1,0:T(2,128)(2,1)S(1)}, u32[]{:S(2)}, u32[]{:S(2)}) collective-permute-start(bf16[1,2048]{1,0:T(2,128)(2,1)S(1)} %convert_element_type.33), channel_id=1, source_target_pairs={{0,4},{4,0},{8,12},{12,8},{1,5},{5,1},{9,13},{13,9},{2,6},{6,2},{1... | collective-permute-start | bytes 12296 | tf_op jit(solution)/shard_map/ppermute | solution.py:17
  38.5 4.6 %collective-permute-start.1 = (bf16[2,2048]{1,0:T(2,128)(2,1)S(1)}, bf16[2,2048]{1,0:T(2,128)(2,1)S(1)}, u32[]{:S(2)}, u32[]{:S(2)}) collective-permute-start(bf16[2,2048]{1,0:T(2,128)(2,1)S(1)} %broadcast_select_fusion), channel_id=1, source_target_pairs={{0,8},{4,12},{8,0},{12,4},{1,9},{5,13},{9,1},{13,5},{2,10},{6,14},... | collective-permute-start | bytes 24584 | tf_op jit(solution)/shard_map/ppermute | solution.py:17
Sparse Core Ops, SparseCore 0:
  22.2 11.7 reduce-scatter.1

commit v2 on v0

--- a/solution.py
+++ b/solution.py
@@ -31,7 +31,8 @@
         jnp.float32
     )
     partial_dec = jnp.dot(scores, table, precision=lax.Precision.HIGHEST)
-    total = lax.psum(partial_dec, ("dp", "tensor", "layer"))
+    answer = jax.lax.all_gather(partial_dec, axis_name=("dp", "tensor", "layer"))
+    total = jnp.sum(answer, 0)
     row = lax.dynamic_slice_in_dim(total, lax.axis_index("dp"), 1, axis=0)
     return row
 

time: 114 us -> 77.5 us (0.68)
  blocking collectives: 76.3 us -> 39.7 us
    psum x1 -> x0, blocking collectives: 57.6 us -> none  [body(): total = lax.psum(partial_dec, ('dp', 'tensor', 'layer'))]
    all_gather x0 -> x1, blocking collectives: none -> 21.1 us  [body(): jax.lax.all_gather(partial_dec, axis_name=('dp', 'tensor', 'layer'))]
where the time goes in v2:
time: 77.5 us; the launch traced here: 77.3 us
  blocking collectives  39.7 us (51%)
  between operations  14.2 us (18%)
  waiting for transfers between devices  11.9 us (15%)
  matrix products  9.12 us (12%)
  local copies, waits for them, and re-layouts  1.48 us (2%)
  other arithmetic  0.78 us (1%)
    all_gather x1, blocking collectives, body(): jax.lax.all_gather(partial_dec, axis_name=('dp', 'tensor', 'layer'))  21.1 us
    all_gather x1, blocking collectives, body(): grads_all = lax.all_gather(grad_flat, 'dp', axis=0, tiled=True)  13.2 us
    reduce_scatter x1, waiting for transfers between devices, body(): lax.psum_scatter(partial, 'tensor', scatter_dimension=0, tiled=True)  11.9 us
    dot_general x1, matrix products, body(): left = jnp.dot(hidden_rows, side_hidden, preferred_element_type=jnp.float32)  5.61 us
    all_gather x1, blocking collectives, body(): right_full = lax.all_gather(right, 'tensor', axis=0, tiled=True)  5.51 us
    dot_general x1, matrix products, body(): right = jnp.dot(grad_rows, side_width, preferred_element_type=jnp.float32)  1.8 us
  transfers between devices with their start and end apart: 1, of which 1 were waited for; matrix products, arithmetic and copies ran while one was open for 0% of the time, Pallas kernels for 0%

profile of v2, /device:TPU:0, one launch (start us, length us, event | category | flops | bytes accessed | tf_op | source)
XLA Modules:
  0.0 77.3 jit_solution(7835386923562751296)
XLA Ops:
  6.5 0.0 copy-start
  6.5 0.0 copy-start.1
  6.5 0.0 copy-start.2
  6.5 0.0 reduce-scatter.2.cloned.1.call-start
  7.4 0.8 %copy-done = bf16[1,1,256,4096]{3,2,1,0:T(8,128)(2,1)S(1)} copy-done((bf16[1,1,256,4096]{3,2,1,0:T(8,128)(2,1)S(1)}, bf16[1,1,256,4096]{3,2,1,0:T(8,128)(2,1)}, u32[]{:S(2)}) %copy-start) | copy-done | bytes 2097176
  8.1 1.8 %fusion.7 = bf16[256,64]{0,1:T(8,128)(2,1)S(1)} fusion(bf16[1,1,256,4096]{3,2,1,0:T(8,128)(2,1)S(1)} %copy-done, bf16[1,4096,64]{1,2,0:T(8,128)(2,1)} %param.10, f32[256]{0:T(256)S(1)} %compare_convert_fusion), kind=kOutput, calls=%fused_computation.5 | convolution fusion | flops 134250496 | bytes 2655232 | tf_op jit(solution)/shard_map/dot_general | solution.py:20
  9.9 5.5 %all_gather.12 = bf16[512,64]{0,1:T(8,128)(2,1)S(1)} all-gather(bf16[256,64]{0,1:T(8,128)(2,1)S(1)} %fusion.7), channel_id=1, replica_groups=mesh['groups'=2,'dp'=4,'tensor'=2,'layer'=2] {'tensor'}, dimensions={0}, use_global_device_ids=true | all-gather | bytes 98304 | tf_op jit(solution)/shard_map/all_gather | solution.py:22
  15.5 5.6 %fusion = f32[512,64]{0,1:T(8,128)S(1)} fusion(bf16[1,1,512,7168]{3,2,1,0:T(8,128)(2,1)} %param.7, bf16[1,7168,64]{1,2,0:T(8,128)(2,1)} %param.9), kind=kOutput, calls=%fused_computation | convolution fusion | flops 469762048 | bytes 8388608 | tf_op jit(solution)/shard_map/dot_general | solution.py:23
  21.1 0.8 %convolution_divide_fusion = f32[64,64]{1,0:T(8,128)} fusion(f32[512,64]{0,1:T(8,128)S(1)} %fusion, bf16[512,64]{0,1:T(8,128)(2,1)S(1)} %all_gather.12, f32[]{:T(128)S(6)} %convert_element_type.31), kind=kOutput, calls=%fused_computation.6 | convolution fusion | flops 25169920 | bytes 212996 | tf_op jit(solution)/shard_map/dot_general | solution.py:24
  21.9 0.0 reduce-scatter.2.cloned.1.call-update
  21.9 11.9 %reduce-scatter.2.cloned.1.call-done = f32[32,64]{1,0:T(8,128)} async-done(((f32[64,64]{1,0:T(8,128)}), f32[32,64]{1,0:T(8,128)}) %reduce-scatter.2.cloned.1.call-update) | async-done | bytes 8208 | tf_op jit(solution)/shard_map/reduce_scatter | solution.py:26
  33.8 0.7 convert_element_type.32
  34.5 0.1 reshape.22
  34.6 13.2 %all-gather.1 = bf16[4,1,2048]{2,1,0:T(2,128)(2,1)S(1)} all-gather(bf16[1,1,2048]{2,1,0:T(2,128)(2,1)S(1)} %reshape.22), channel_id=1, replica_groups=mesh['groups'=2,'dp'=4,'tensor'=2,'layer'=2] {'dp'}, dimensions={0}, use_global_device_ids=true | all-gather | bytes 20480 | tf_op jit(solution)/shard_map/all_gather | solution.py:28
  47.8 0.0 copy-done.1
  47.8 0.4 fusion.10
  48.2 0.0 copy-done.2
  48.2 0.5 convolution_bitcast_fusion
  48.7 21.1 %all-gather.2 = f32[16,4,1024]{2,1,0:T(4,128)S(1)} all-gather(f32[1,4,1024]{2,1,0:T(4,128)S(1)} %convolution_bitcast_fusion), channel_id=2, replica_groups=mesh['groups'=2,'dp'=4,'tensor'=2,'layer'=2] {'dp','tensor','layer'}, dimensions={0}, use_global_device_ids=true | all-gather | bytes 278528 | tf_op jit(solution)/shard_map/all_gather | solution.py:34
  69.8 0.1 reduce_sum.9
  69.8 0.6 constant_dynamic-slice_fusion
  (1 shorter events, 0.0 us)
Async XLA Ops:
  6.5 1.6 %copy-start = (bf16[1,1,256,4096]{3,2,1,0:T(8,128)(2,1)S(1)}, bf16[1,1,256,4096]{3,2,1,0:T(8,128)(2,1)}, u32[]{:S(2)}) copy-start(bf16[1,1,256,4096]{3,2,1,0:T(8,128)(2,1)} %param.8) | copy-start | bytes 6291460
  6.5 41.2 %copy-start.1 = (bf16[1,256,2048]{2,1,0:T(8,128)(2,1)S(1)}, bf16[1,256,2048]{2,1,0:T(8,128)(2,1)}, u32[]{:S(2)}) copy-start(bf16[1,256,2048]{2,1,0:T(8,128)(2,1)} %param.11) | copy-start | bytes 3145732
  6.5 41.6 %copy-start.2 = (s32[256]{0:T(256)S(1)}, s32[256]{0:T(256)}, u32[]{:S(2)}) copy-start(s32[256]{0:T(256)} %param.13) | copy-start | bytes 3076
  6.5 27.3 %reduce-scatter.2.cloned.1.call-start = ((), (), s32[]{:S(2)}) async-start(), calls=%async_computation.1 | async-start | bytes 49152 | tf_op jit(solution)/shard_map/reduce_scatter | solution.py:26
Sparse Core Ops, SparseCore 0:
  22.0 11.7 reduce-scatter.1
